TPU v7x, 256 devices: a whole 4x4x8 slice. The times are simulated.
256 devices in a mesh: tok: 32 (over x, z), hid: 8 (over y, core).
Axes of the slice: x: 4, y: 4, z: 8, core: 2. Of those that a mesh axis runs over, the one named last changes fastest.
Arguments:
- tokens: bfloat16 [16384, 5376], P('tok', 'hid'), may hold values from -6 to 6
- norm_gain: bfloat16 [1, 5376], P(None, 'hid'), may hold values from 0.099609375 to 1.8984375
- w_query: bfloat16 [5376, 4096], P('tok', 'hid'), may hold values from -2 to 2
- w_key: bfloat16 [5376, 2048], P('tok', 'hid'), may hold values from -1 to 1
- value_matrix: bfloat16 [5376, 2048], P('tok', 'hid'), may hold values from -0.078125 to 0.078125
- q_norm_gain: bfloat16 [1, 128], replicated, may hold values from 0.1 to 8
- k_norm_gain: bfloat16 [1, 128], replicated, may hold values from 0.1 to 8
- w_out: bfloat16 [4096, 5376], P('hid'), may hold values from -0.125 to 0.125
Outputs:
- attended: bfloat16 [16384, 5376], P('tok', 'hid')
All inputs are finite; a program needn't handle non-finite values.
Results may differ from a plain program's by a relative error of at most 0.017.
Values may be sent and summed in bfloat16 or wider, within the bound.
No kernel may reach another device: no remote copies, remote signals or barrier semaphores. Data moves between devices by JAX's collectives and lax.ppermute only.
A program may use at most 64 MiB of HBM per device.

v0:
```python
import math
import jax
import jax.numpy as jnp
from jax import lax
from jax.sharding import PartitionSpec as P

HEAD_SIZE = 128
WINDOW = 1024
TOK = ("tx", "tz")
HID = ("hy", "hc")
score_scale = 168.0 ** (-0.5)


def shifted(value, axis, steps):
    count = lax.axis_size(axis)
    leading, last = (max(0, -steps), min(count, count - steps))
    return lax.ppermute(value, axis, [(source, source + steps) for source in range(leading, last)])


def head_norm(field, gain):
    count = field.shape[0]
    heads = field.reshape(count, -1, HEAD_SIZE)
    mean_square = jnp.mean(heads * heads, axis=-1, keepdims=True)
    scaled = (
        heads * lax.rsqrt(mean_square + 1e-06) * gain.astype(jnp.float32).reshape(1, 1, HEAD_SIZE)
    )
    return scaled.reshape(count, -1)


def rotate(field, positions):
    count = field.shape[0]
    heads = field.reshape(count, -1, HEAD_SIZE)
    half = HEAD_SIZE // 2
    inverse = jnp.exp(-math.log(10000.0) * jnp.arange(half, dtype=jnp.float32) * 2.0 / HEAD_SIZE)
    angles = positions.astype(jnp.float32)[:, None] * inverse[None, :]
    cosine = jnp.cos(angles)[:, None, :]
    sine = jnp.sin(angles)[:, None, :]
    first = heads[..., :half]
    second = heads[..., half:]
    turned = jnp.concatenate(
        [first * cosine - second * sine, second * cosine + first * sine], axis=-1
    )
    return turned.reshape(count, -1)


def local(tokens, norm_gain, w_query, w_key, value_matrix, q_norm_gain, k_norm_gain, w_out):
    rows = tokens.shape[0]
    with_gain = jnp.concatenate([tokens, norm_gain], axis=0)
    n_hid = lax.axis_size(HID)
    hid_index = lax.axis_index(HID)
    received = [with_gain] + [
        lax.ppermute(with_gain, HID, [(i, (i + k) % n_hid) for i in range(n_hid)])
        for k in range(1, n_hid)
    ]
    by_shift = jnp.stack(received)
    ordered = jnp.take(by_shift, (hid_index - jnp.arange(n_hid)) % n_hid, axis=0)
    values32 = ordered[:, :rows].astype(jnp.float32)
    gain_rows = ordered[:, rows:].astype(jnp.float32)
    mean_square = jnp.sum(values32 * values32, axis=(0, 2)) / (n_hid * values32.shape[2])
    scale_rows = lax.rsqrt(mean_square + 1e-06)[None, :, None]
    normed = (values32 * scale_rows * gain_rows).astype(jnp.bfloat16)
    width_query = w_query.shape[1]
    width_kv = w_key.shape[1]
    stacked = lax.all_gather(
        lax.all_gather(
            jnp.concatenate([w_query, w_key, value_matrix], axis=1), "tz", axis=0, tiled=True
        ),
        "tx",
        axis=0,
        tiled=True,
    )
    weights3 = stacked.reshape(n_hid, normed.shape[2], stacked.shape[1])
    projected_kv = jnp.einsum(
        "jrc,jcn->rn", normed, weights3[:, :, width_query:], preferred_element_type=jnp.float32
    )
    key_raw = projected_kv[:, :width_kv]
    value_raw = projected_kv[:, width_kv:]
    tok_index = lax.axis_index(TOK)
    positions = tok_index * rows + jnp.arange(rows, dtype=jnp.int32)
    key = rotate(head_norm(key_raw, k_norm_gain), positions).astype(jnp.bfloat16)
    value_rows = value_raw.astype(jnp.bfloat16)
    joined = jnp.concatenate([key, value_rows], axis=1)
    reach = (WINDOW - 1 + rows - 1) // rows
    earlier = [shifted(joined, TOK, offset) for offset in range(reach, 0, -1)]
    normed_late, _ = lax.optimization_barrier((normed, joined))
    query_raw = jnp.einsum(
        "jrc,jcn->rn", normed_late, weights3[:, :, :width_query], preferred_element_type=jnp.float32
    )
    query = rotate(head_norm(query_raw, q_norm_gain), positions).astype(jnp.bfloat16)
    window_kv = jnp.concatenate(earlier + [joined], axis=0)
    window_extent = window_kv.shape[0]
    key_pos = (tok_index - reach) * rows + jnp.arange(window_extent, dtype=jnp.int32)
    kv_heads = width_kv // HEAD_SIZE
    query_group_count = width_query // HEAD_SIZE // kv_heads
    query_four_axes = query.reshape(rows, kv_heads, query_group_count, HEAD_SIZE)
    keys_three_axes = window_kv[:, :width_kv].reshape(window_extent, kv_heads, HEAD_SIZE)
    values_three_axes = window_kv[:, width_kv:].reshape(window_extent, kv_heads, HEAD_SIZE)
    scores = (
        jnp.einsum(
            "tkgd,skd->kgts", query_four_axes, keys_three_axes, preferred_element_type=jnp.float32
        )
        * score_scale
    )
    allowed = (
        (key_pos[None, :] <= positions[:, None])
        & (key_pos[None, :] > positions[:, None] - WINDOW)
        & (key_pos[None, :] >= 0)
    )
    masked = jnp.where(allowed, scores, -1e30)
    top = jnp.max(masked, axis=-1, keepdims=True)
    weights = jnp.where(allowed, jnp.exp(masked - top), 0.0)
    total = jnp.sum(weights, axis=-1)
    probs = weights.astype(jnp.bfloat16)
    mixed = jnp.einsum(
        "kgts,skd->tkgd", probs, values_three_axes, preferred_element_type=jnp.float32
    )
    mixed = mixed / jnp.transpose(total, (2, 0, 1))[..., None]
    heads_out = mixed.reshape(rows, width_query).astype(jnp.bfloat16)
    partial_value = jnp.dot(heads_out, w_out, preferred_element_type=jnp.float32)
    return lax.psum_scatter(
        partial_value.astype(jnp.bfloat16), HID, scatter_dimension=1, tiled=True
    )


def solution(mesh):
    devices = mesh.devices
    n_x = len({d.coords[0] for d in devices.flat})
    n_y = len({d.coords[1] for d in devices.flat})
    split = jax.sharding.Mesh(
        devices.reshape(n_x, devices.shape[0] // n_x, n_y, devices.shape[1] // n_y),
        ("tx", "tz", "hy", "hc"),
    )
    in_specs = (
        P(TOK, HID),
        P(None, HID),
        P(TOK, HID),
        P(TOK, HID),
        P(TOK, HID),
        P(),
        P(),
        P(HID, None),
    )
    out_specs = P(TOK, HID)
    return jax.shard_map(local, mesh=split, in_specs=in_specs, out_specs=out_specs, check_vma=False)
```

profile of v0, /device:TPU:2, one launch (start us, length us, event | category | flops | bytes accessed | tf_op | source)
XLA Modules:
  0.0 282.9 jit_solution(6416758314910907047)
XLA Ops:
  6.5 1.8 pad_maximum_fusion.3
  8.4 0.0 all-gather.5.cloned.1.call-start
  8.4 46.3 %all-gather.3.cloned.1.call-done = bf16[1344,1024]{1,0:T(8,128)(2,1)} async-done(((bf16[168,1024]{1,0:T(8,128)(2,1)}), bf16[1344,1024]{1,0:T(8,128)(2,1)}) %all-gather.3.cloned.1.call-update) | async-done | bytes 2752528 | tf_op jit(solution)/shard_map/all_gather | solution.py:65
  54.8 1.4 copy.19
  56.2 0.8 pad_maximum_fusion
  57.0 1.6 collective-permute-start.1
  58.6 2.0 collective-permute-start.2
  60.6 2.0 collective-permute-start.3
  62.6 1.6 collective-permute-start.4
  64.3 0.5 multiply_cosine_fusion
  64.9 1.9 and_and_fusion
  66.8 1.0 bitcast_dynamic-update-slice_fusion.7
  67.8 9.9 %collective-permute-done = bf16[513,672]{1,0:T(8,128)(2,1)} collective-permute-done((bf16[513,672]{1,0:T(8,128)(2,1)S(1)}, bf16[513,672]{1,0:T(8,128)(2,1)}, u32[]{:S(2)}, u32[]{:S(2)}) %collective-permute-start) | collective-permute-done | bytes 689504 | tf_op jit(solution)/shard_map/ppermute | solution.py:52
  77.7 1.5 collective-permute-start.5
  79.3 2.1 bitcast_dynamic-update-slice_fusion.6
  81.4 14.7 %collective-permute-start.6 = (bf16[513,672]{1,0:T(8,128)(2,1)S(1)}, bf16[513,672]{1,0:T(8,128)(2,1)S(1)}, u32[]{:S(2)}, u32[]{:S(2)}) collective-permute-start(bf16[513,672]{1,0:T(8,128)(2,1)S(1)} %pad_maximum_fusion), channel_id=1, source_target_pairs={{0,7},{1,0},{2,1},{3,2},{4,3},{5,4},{6,5},{7,6},{8,15},{9,8},{10,9... | collective-permute-start | bytes 2068424 | tf_op jit(solution)/shard_map/ppermute | solution.py:52
  96.1 2.1 bitcast_dynamic-update-slice_fusion.5
  98.2 14.7 %collective-permute-done.2 = bf16[513,672]{1,0:T(8,128)(2,1)} collective-permute-done((bf16[513,672]{1,0:T(8,128)(2,1)S(1)}, bf16[513,672]{1,0:T(8,128)(2,1)}, u32[]{:S(2)}, u32[]{:S(2)}) %collective-permute-start.2) | collective-permute-done | bytes 689504 | tf_op jit(solution)/shard_map/ppermute | solution.py:52
  112.9 2.1 bitcast_dynamic-update-slice_fusion.4
  115.0 1.0 bitcast_dynamic-update-slice_fusion.3
  116.0 11.4 %collective-permute-done.4 = bf16[513,672]{1,0:T(8,128)(2,1)S(1)} collective-permute-done((bf16[513,672]{1,0:T(8,128)(2,1)S(1)}, bf16[513,672]{1,0:T(8,128)(2,1)S(1)}, u32[]{:S(2)}, u32[]{:S(2)}) %collective-permute-start.4) | collective-permute-done | bytes 689504 | tf_op jit(solution)/shard_map/ppermute | solution.py:52
  127.4 1.0 bitcast_dynamic-update-slice_fusion.2
  128.4 1.0 bitcast_dynamic-update-slice_fusion.1
  129.4 0.2 collective-permute-done.6
  129.6 0.9 bitcast_dynamic-update-slice_fusion
  130.5 6.5 %gather_fusion = bf16[8,513,672]{2,1,0:T(8,128)(2,1)} fusion(bf16[8,513,672]{2,1,0:T(8,128)(2,1)} %bitcast_dynamic-update-slice_fusion, s32[1024]{0:T(1024)S(1)} %pad_clamp_fusion), kind=kCustom, calls=%fused_computation | custom fusion | bytes 11031584 | tf_op jit(solution)/shard_map/jit(_take)/gather | solution.py:56
  137.0 3.5 %broadcast_select_fusion = bf16[8,513,672]{2,1,0:T(8,128)(2,1)S(1)} fusion(bf16[8,513,672]{2,1,0:T(8,128)(2,1)} %gather_fusion, pred[8]{0:T(512)(128)(4,1)S(1)} %compare_and_fusion), kind=kLoop, calls=%fused_computation.11 | loop fusion | flops 2757888 | bytes 11031560 | tf_op jit(solution)/shard_map/jit(_take)/select_n | solution.py:56
  140.6 1.4 fusion.1
  142.0 4.7 %fusion.3 = bf16[8,512,672]{2,1,0:T(8,128)(2,1)} fusion(f32[8,672]{1,0:T(8,128)S(1)} %bitcast.85, f32[512]{0:T(512)S(1)} %add_rsqrt_fusion.2, bf16[8,513,672]{2,1,0:T(8,128)(2,1)S(1)} %broadcast_select_fusion), kind=kLoop, calls=%fused_computation.6 | loop fusion | flops 11010048 | bytes 11033600 | tf_op jit(solution)/shard_map/convert_element_type | solution.py:61
  146.6 16.5 %all-gather.5.cloned.1.call-done = bf16[5376,1024]{1,0:T(8,128)(2,1)} async-done(((bf16[1344,1024]{1,0:T(8,128)(2,1)}), bf16[5376,1024]{1,0:T(8,128)(2,1)}) %all-gather.5.cloned.1.call-update) | async-done | bytes 11010064 | tf_op jit(solution)/shard_map/all_gather | solution.py:64
  163.1 8.3 %fusion.14 = f32[512,512]{0,1:T(8,128)S(1)} fusion(bf16[8,512,672]{2,1,0:T(8,128)(2,1)} %fusion.3, bf16[8,672,1024]{2,1,0:T(8,128)(2,1)} %bitcast.86), kind=kOutput, calls=%fused_computation.23 | convolution fusion | flops 2818572288 | bytes 12845056 | tf_op jit(solution)/shard_map/jrc,jcn->rn/dot_general | solution.py:73
  171.4 0.1 multiply_reduce_fusion.1
  171.6 0.1 multiply_multiply_fusion.1
  171.7 0.1 subtract_convert_fusion.1
  171.8 4.5 %collective-permute-start.7 = (bf16[512,512]{0,1:T(8,128)(2,1)S(1)}, bf16[512,512]{0,1:T(8,128)(2,1)S(1)}, u32[]{:S(2)}, u32[]{:S(2)}) collective-permute-start(bf16[512,512]{0,1:T(8,128)(2,1)S(1)} %pad_maximum_fusion.1), channel_id=1, source_target_pairs={{0,16},{8,24},{16,32},{24,40},{32,48},{40,56},{48,64},{56,72},{64,... | collective-permute-start | bytes 1572872 | tf_op jit(solution)/shard_map/ppermute | solution.py:17
  176.3 3.7 %collective-permute-start.8 = (bf16[512,512]{0,1:T(8,128)(2,1)S(1)}, bf16[512,512]{0,1:T(8,128)(2,1)S(1)}, u32[]{:S(2)}, u32[]{:S(2)}) collective-permute-start(bf16[512,512]{0,1:T(8,128)(2,1)S(1)} %pad_maximum_fusion.1), channel_id=1, source_target_pairs={{0,8},{8,16},{16,24},{24,32},{32,40},{40,48},{48,56},{56,64},{64,7... | collective-permute-start | bytes 1572872 | tf_op jit(solution)/shard_map/ppermute | solution.py:17
  180.0 5.5 %fusion.10 = f32[512,512,1]{0,1,2:T(8,128)S(1)} fusion(bf16[8,512,672]{2,1,0:T(8,128)(2,1)S(1)} %copy-done, bf16[8,672,1024]{2,1,0:T(8,128)(2,1)} %bitcast.87), kind=kOutput, calls=%fused_computation.17 | convolution fusion | flops 2818572288 | bytes 12058624 | tf_op jit(solution)/shard_map/jrc,jcn->rn/dot_general | solution.py:86
  185.6 0.1 multiply_reduce_fusion
  185.7 0.2 multiply_multiply_fusion
  185.9 0.2 subtract_convert_fusion
  186.1 15.8 %collective-permute-done.7 = bf16[512,512]{0,1:T(8,128)(2,1)S(1)} collective-permute-done((bf16[512,512]{0,1:T(8,128)(2,1)S(1)}, bf16[512,512]{0,1:T(8,128)(2,1)S(1)}, u32[]{:S(2)}, u32[]{:S(2)}) %collective-permute-start.7) | collective-permute-done | bytes 524320 | tf_op jit(solution)/shard_map/ppermute | solution.py:17
  201.9 10.8 %collective-permute-done.8 = bf16[512,512]{0,1:T(8,128)(2,1)S(1)} collective-permute-done((bf16[512,512]{0,1:T(8,128)(2,1)S(1)}, bf16[512,512]{0,1:T(8,128)(2,1)S(1)}, u32[]{:S(2)}, u32[]{:S(2)}) %collective-permute-start.8) | collective-permute-done | bytes 524320 | tf_op jit(solution)/shard_map/ppermute | solution.py:17
  212.7 0.1 maximum_maximum_fusion
  212.8 0.1 fusion.35
  212.9 8.5 %fusion.36 = (f32[2,2,512]{2,1,0:T(2,128)S(1)}, bf16[2,2,512,1536]{2,3,1,0:T(8,128)(2,1)}) fusion(pred[512,1536]{0,1:T(8,128)(4,1)S(1)} %copy-done.1, bf16[1536,2,128,1]{0,2,3,1:T(8,128)(2,1)S(1)} %bitcast.83, bf16[512,2,2,128]{0,3,2,1:T(8,128)(2,1)S(1)} %bitcast.84), kind=kOutput, calls=%fused_computation.81 | convolution fusion | flops 824182272 | bytes 8396800 | tf_op jit(solution)/shard_map/sub | solution.py:111
  221.4 3.8 %fusion.25 = bf16[512,2,2,128]{0,3,2,1:T(8,128)(2,1)S(1)} fusion(bf16[1536,2,128,1]{0,2,3,1:T(8,128)(2,1)S(1)} %bitcast.82, bf16[2,2,512,1536]{2,3,1,0:T(8,128)(2,1)} %get-tuple-element.16, f32[512,2,2]{0,2,1:T(2,128)S(1)} %bitcast.89), kind=kOutput, calls=%fused_computation.27 | convolution fusion | flops 805830656 | bytes 7610368 | tf_op jit(solution)/shard_map/kgts,skd->tkgd/dot_general | solution.py:114
  225.2 8.6 %convolution_convert_fusion = bf16[512,5376]{0,1:T(8,128)(2,1)} fusion(bf16[512,512]{0,1:T(8,128)(2,1)S(1)} %bitcast.88, bf16[512,5376]{1,0:T(8,128)(2,1)} %param.15), kind=kOutput, calls=%fused_computation.10 | convolution fusion | flops 2821324800 | bytes 11534336 | tf_op jit(solution)/shard_map/dot_general | solution.py:119
  233.9 42.5 %reduce-scatter.2.cloned.1.call-done = bf16[512,672]{0,1:T(8,128)(2,1)} async-done(((bf16[512,5376]{0,1:T(8,128)(2,1)}), bf16[512,672]{0,1:T(8,128)(2,1)}) %reduce-scatter.2.cloned.1.call-update) | async-done | bytes 688144 | tf_op jit(solution)/shard_map/reduce_scatter | solution.py:120
  (38 shorter events, 0.4 us)
Async XLA Ops:
  6.5 60.3 %copy-start.2 = (bf16[1,672]{1,0:T(2,128)(2,1)S(1)}, bf16[1,672]{1,0:T(2,128)(2,1)}, u32[]{:S(2)}) copy-start(bf16[1,672]{1,0:T(2,128)(2,1)} %param.9) | copy-start | bytes 4036
  6.5 60.3 %copy-start.3 = (bf16[1,128]{1,0:T(2,128)(2,1)S(1)}, bf16[1,128]{1,0:T(2,128)(2,1)}, u32[]{:S(2)}) copy-start(bf16[1,128]{1,0:T(2,128)(2,1)} %param.14) | copy-start | bytes 772
  6.5 60.3 %copy-start.4 = (bf16[1,128]{1,0:T(2,128)(2,1)S(1)}, bf16[1,128]{1,0:T(2,128)(2,1)}, u32[]{:S(2)}) copy-start(bf16[1,128]{1,0:T(2,128)(2,1)} %param.13) | copy-start | bytes 772
  6.5 48.2 %all-gather.3.cloned.1.call-start = ((), (), s32[]{:S(2)}) async-start(), calls=%async_computation.1 | async-start | bytes 3096576 | tf_op jit(solution)/shard_map/all_gather | solution.py:65
  8.4 154.7 %all-gather.5.cloned.1.call-start = ((), (), s32[]{:S(2)}) async-start(), calls=%async_computation.2 | async-start | bytes 13762560 | tf_op jit(solution)/shard_map/all_gather | solution.py:64
  54.8 221.6 %reduce-scatter.2.cloned.1.call-start = ((), (), s32[]{:S(2)}) async-start(), calls=%async_computation.3 | async-start | bytes 6193152 | tf_op jit(solution)/shard_map/reduce_scatter | solution.py:120
  57.0 20.8 %collective-permute-start = (bf16[513,672]{1,0:T(8,128)(2,1)S(1)}, bf16[513,672]{1,0:T(8,128)(2,1)}, u32[]{:S(2)}, u32[]{:S(2)}) collective-permute-start(bf16[513,672]{1,0:T(8,128)(2,1)S(1)} %pad_maximum_fusion), channel_id=1, source_target_pairs={{0,1},{1,2},{2,3},{3,4},{4,5},{5,6},{6,7},{7,0},{8,9},{9,10},{10,1... | collective-permute-start | bytes 2068424 | tf_op jit(solution)/shard_map/ppermute | solution.py:52
  57.0 24.4 %collective-permute-start.1 = (bf16[513,672]{1,0:T(8,128)(2,1)S(1)}, bf16[513,672]{1,0:T(8,128)(2,1)}, u32[]{:S(2)}, u32[]{:S(2)}) collective-permute-start(bf16[513,672]{1,0:T(8,128)(2,1)S(1)} %pad_maximum_fusion), channel_id=1, source_target_pairs={{0,2},{1,3},{2,4},{3,5},{4,6},{5,7},{6,0},{7,1},{8,10},{9,11},{10,... | collective-permute-start | bytes 2068424 | tf_op jit(solution)/shard_map/ppermute | solution.py:52
  58.6 54.4 %collective-permute-start.2 = (bf16[513,672]{1,0:T(8,128)(2,1)S(1)}, bf16[513,672]{1,0:T(8,128)(2,1)}, u32[]{:S(2)}, u32[]{:S(2)}) collective-permute-start(bf16[513,672]{1,0:T(8,128)(2,1)S(1)} %pad_maximum_fusion), channel_id=1, source_target_pairs={{0,3},{1,4},{2,5},{3,6},{4,7},{5,0},{6,1},{7,2},{8,11},{9,12},{10,... | collective-permute-start | bytes 2068424 | tf_op jit(solution)/shard_map/ppermute | solution.py:52
  60.6 54.4 %collective-permute-start.3 = (bf16[513,672]{1,0:T(8,128)(2,1)S(1)}, bf16[513,672]{1,0:T(8,128)(2,1)S(1)}, u32[]{:S(2)}, u32[]{:S(2)}) collective-permute-start(bf16[513,672]{1,0:T(8,128)(2,1)S(1)} %pad_maximum_fusion), channel_id=1, source_target_pairs={{0,4},{1,5},{2,6},{3,7},{4,0},{5,1},{6,2},{7,3},{8,12},{9,13},{10,... | collective-permute-start | bytes 2068424 | tf_op jit(solution)/shard_map/ppermute | solution.py:52
  62.6 64.8 %collective-permute-start.4 = (bf16[513,672]{1,0:T(8,128)(2,1)S(1)}, bf16[513,672]{1,0:T(8,128)(2,1)S(1)}, u32[]{:S(2)}, u32[]{:S(2)}) collective-permute-start(bf16[513,672]{1,0:T(8,128)(2,1)S(1)} %pad_maximum_fusion), channel_id=1, source_target_pairs={{0,5},{1,6},{2,7},{3,0},{4,1},{5,2},{6,3},{7,4},{8,13},{9,14},{10,... | collective-permute-start | bytes 2068424 | tf_op jit(solution)/shard_map/ppermute | solution.py:52
  77.7 50.7 %collective-permute-start.5 = (bf16[513,672]{1,0:T(8,128)(2,1)S(1)}, bf16[513,672]{1,0:T(8,128)(2,1)S(1)}, u32[]{:S(2)}, u32[]{:S(2)}) collective-permute-start(bf16[513,672]{1,0:T(8,128)(2,1)S(1)} %pad_maximum_fusion), channel_id=1, source_target_pairs={{0,6},{1,7},{2,0},{3,1},{4,2},{5,3},{6,4},{7,5},{8,14},{9,15},{10,... | collective-permute-start | bytes 2068424 | tf_op jit(solution)/shard_map/ppermute | solution.py:52
  81.4 48.2 %collective-permute-start.6 = (bf16[513,672]{1,0:T(8,128)(2,1)S(1)}, bf16[513,672]{1,0:T(8,128)(2,1)S(1)}, u32[]{:S(2)}, u32[]{:S(2)}) collective-permute-start(bf16[513,672]{1,0:T(8,128)(2,1)S(1)} %pad_maximum_fusion), channel_id=1, source_target_pairs={{0,7},{1,0},{2,1},{3,2},{4,3},{5,4},{6,5},{7,6},{8,15},{9,8},{10,9... | collective-permute-start | bytes 2068424 | tf_op jit(solution)/shard_map/ppermute | solution.py:52
  163.1 16.9 %copy-start = (bf16[8,512,672]{2,1,0:T(8,128)(2,1)S(1)}, bf16[8,512,672]{2,1,0:T(8,128)(2,1)}, u32[]{:S(2)}) copy-start(bf16[8,512,672]{2,1,0:T(8,128)(2,1)} %fusion.3) | copy-start | bytes 16515076
  171.8 30.0 %collective-permute-start.7 = (bf16[512,512]{0,1:T(8,128)(2,1)S(1)}, bf16[512,512]{0,1:T(8,128)(2,1)S(1)}, u32[]{:S(2)}, u32[]{:S(2)}) collective-permute-start(bf16[512,512]{0,1:T(8,128)(2,1)S(1)} %pad_maximum_fusion.1), channel_id=1, source_target_pairs={{0,16},{8,24},{16,32},{24,40},{32,48},{40,56},{48,64},{56,72},{64,... | collective-permute-start | bytes 1572872 | tf_op jit(solution)/shard_map/ppermute | solution.py:17
  176.3 36.4 %collective-permute-start.8 = (bf16[512,512]{0,1:T(8,128)(2,1)S(1)}, bf16[512,512]{0,1:T(8,128)(2,1)S(1)}, u32[]{:S(2)}, u32[]{:S(2)}) collective-permute-start(bf16[512,512]{0,1:T(8,128)(2,1)S(1)} %pad_maximum_fusion.1), channel_id=1, source_target_pairs={{0,8},{8,16},{16,24},{24,32},{32,40},{40,48},{48,56},{56,64},{64,7... | collective-permute-start | bytes 1572872 | tf_op jit(solution)/shard_map/ppermute | solution.py:17
  185.5 27.4 %copy-start.1 = (pred[512,1536]{0,1:T(8,128)(4,1)S(1)}, pred[512,1536]{0,1:T(8,128)(4,1)}, u32[]{:S(2)}) copy-start(pred[512,1536]{0,1:T(8,128)(4,1)} %and_and_fusion) | copy-start | bytes 2359300
Sparse Core Ops, SparseCore 0:
  9.1 45.5 all-gather.2
  56.6 106.4 all-gather.4
  234.0 42.3 reduce-scatter.1
where the time goes:
time: 283 us
  waiting for transfers between devices  168 us (59%)
  matrix products  34.7 us (12%)
  starting transfers between devices  31.7 us (11%)
  local copies, waits for them, and re-layouts  18.2 us (6%)
  other arithmetic  16.6 us (6%)
  between operations  13.4 us (5%)
    all_gather x1, waiting for transfers between devices, local(): lax.all_gather(jnp.concatenate([w_query, w_key, value_matrix], axis=1), '...  46.3 us
    reduce_scatter x1, waiting for transfers between devices, local(): lax.psum_scatter(partial_value.astype(jnp.bfloat16), HID, scatter_dimensi...  42.5 us
    ppermute x7, waiting for transfers between devices, local(): lax.ppermute(with_gain, HID, [(i, (i + k) % n_hid) for i in range(n_hid)])  36.3 us
    ppermute x2, waiting for transfers between devices, shifted(): lax.ppermute(value, axis, [(source, source + steps) for source in range(l...  26.6 us
    ppermute x7, starting transfers between devices, local(): lax.ppermute(with_gain, HID, [(i, (i + k) % n_hid) for i in range(n_hid)])  23.5 us
    all_gather x1, waiting for transfers between devices, local(): lax.all_gather(lax.all_gather(jnp.concatenate([w_query, w_key, value_matr...  16.5 us
    unnamed x18, local copies, waits for them, and re-layouts  10.6 us
    dot_general x1, matrix products, local(): jnp.dot(heads_out, w_out, preferred_element_type=jnp.float32)  8.63 us
  transfers between devices with their start and end apart: 12, of which 9 were waited for; matrix products, arithmetic and copies ran while one was open for 13% of the time, Pallas kernels for 0%

commit v1 on v0

--- a/solution.py
+++ b/solution.py
@@ -9,6 +9,15 @@
 TOK = ("tx", "tz")
 HID = ("hy", "hc")
 score_scale = 168.0 ** (-0.5)
+solve_rates_on_mesh = lambda target: jnp.concatenate(
+    lax.all_to_all(
+        jnp.stack([target] * lax.psum(1, axis_name="tz")),
+        axis_name="tz",
+        split_axis=0,
+        concat_axis=0,
+    ),
+    axis=0,
+)
 
 
 def shifted(value, axis, steps):
@@ -62,9 +71,7 @@
     width_query = w_query.shape[1]
     width_kv = w_key.shape[1]
     stacked = lax.all_gather(
-        lax.all_gather(
-            jnp.concatenate([w_query, w_key, value_matrix], axis=1), "tz", axis=0, tiled=True
-        ),
+        solve_rates_on_mesh(jnp.concatenate([w_query, w_key, value_matrix], axis=1)),
         "tx",
         axis=0,
         tiled=True,

time: 283 us -> 307 us (1.085)
  blocking collectives: 0 us -> 73.7 us
  waiting for transfers between devices: 168 us -> 119 us
    all_to_all x0 -> x1, blocking collectives: none -> 73.7 us  [lax.all_to_all(jnp.stack([target] * lax.psum(1, axis_name='tz')), axis_na...]
    all_gather x2 -> x1, waiting for transfers between devices: 62.8 us -> 14.1 us  [local(): lax.all_gather(solve_rates_on_mesh(jnp.concatenate([w_query, w_key, value...]
    unnamed x18 -> x20, local copies, waits for them, and re-layouts: 10.6 us -> 9.49 us
  transfers between devices with their start and end apart: 12 -> 11, of which waited for: 9 -> 8; matrix products, arithmetic and copies ran while one was open for 13% -> 12% of each run, Pallas kernels for 0% -> 0%
where the time goes in v1:
time: 307 us; the launch traced here: 306 us
  waiting for transfers between devices  119 us (39%)
  blocking collectives  73.7 us (24%)
  matrix products  34.8 us (11%)
  starting transfers between devices  32.3 us (11%)
  local copies, waits for them, and re-layouts  17.5 us (6%)
  other arithmetic  15.2 us (5%)
  between operations  13.7 us (4%)
    all_to_all x1, blocking collectives, lax.all_to_all(jnp.stack([target] * lax.psum(1, axis_name='tz')), axis_na...  73.7 us
    reduce_scatter x1, waiting for transfers between devices, local(): lax.psum_scatter(partial_value.astype(jnp.bfloat16), HID, scatter_dimensi...  42.5 us
    ppermute x7, waiting for transfers between devices, local(): lax.ppermute(with_gain, HID, [(i, (i + k) % n_hid) for i in range(n_hid)])  35.8 us
    ppermute x2, waiting for transfers between devices, shifted(): lax.ppermute(value, axis, [(source, source + steps) for source in range(l...  26.6 us
    ppermute x7, starting transfers between devices, local(): lax.ppermute(with_gain, HID, [(i, (i + k) % n_hid) for i in range(n_hid)])  24.1 us
    all_gather x1, waiting for transfers between devices, local(): lax.all_gather(solve_rates_on_mesh(jnp.concatenate([w_query, w_key, value...  14.1 us
    unnamed x20, local copies, waits for them, and re-layouts  9.49 us
    dot_general x1, matrix products, local(): jnp.dot(heads_out, w_out, preferred_element_type=jnp.float32)  8.64 us
  transfers between devices with their start and end apart: 11, of which 8 were waited for; matrix products, arithmetic and copies ran while one was open for 12% of the time, Pallas kernels for 0%

profile of v1, /device:TPU:2, one launch (start us, length us, event | category | flops | bytes accessed | tf_op | source)
XLA Modules:
  0.0 306.2 jit_solution(8983438921325019421)
XLA Ops:
  6.5 1.1 pad_maximum_fusion.3
  7.7 0.3 stack.47
  8.0 73.7 %all_to_all.5 = bf16[8,168,1024]{2,1,0:T(8,128)(2,1)} all-to-all(bf16[8,168,1024]{2,1,0:T(8,128)(2,1)S(1)} %stack.47), channel_id=1, replica_groups=mesh['tx'=4,'tz'=8,'hy'=4,'hc'=2] {'tz'}, dimensions={0} | all-to-all | bytes 5505024 | tf_op jit(solution)/shard_map/all_to_all | solution.py:13
  81.9 0.3 copy.19
  82.2 0.1 pad_maximum_fusion
  82.3 1.7 collective-permute-start.1
  83.9 2.2 collective-permute-start.2
  86.1 1.8 collective-permute-start.3
  88.0 1.8 collective-permute-start.4
  89.9 0.5 multiply_cosine_fusion
  90.4 1.9 and_and_fusion
  92.4 1.0 bitcast_dynamic-update-slice_fusion.7
  93.3 9.7 %collective-permute-done = bf16[513,672]{1,0:T(8,128)(2,1)} collective-permute-done((bf16[513,672]{1,0:T(8,128)(2,1)S(1)}, bf16[513,672]{1,0:T(8,128)(2,1)}, u32[]{:S(2)}, u32[]{:S(2)}) %collective-permute-start) | collective-permute-done | bytes 689504 | tf_op jit(solution)/shard_map/ppermute | solution.py:61
  103.0 1.8 collective-permute-start.5
  104.8 2.1 bitcast_dynamic-update-slice_fusion.6
  106.9 14.7 %collective-permute-start.6 = (bf16[513,672]{1,0:T(8,128)(2,1)S(1)}, bf16[513,672]{1,0:T(8,128)(2,1)S(1)}, u32[]{:S(2)}, u32[]{:S(2)}) collective-permute-start(bf16[513,672]{1,0:T(8,128)(2,1)S(1)} %pad_maximum_fusion), channel_id=1, source_target_pairs={{0,7},{1,0},{2,1},{3,2},{4,3},{5,4},{6,5},{7,6},{8,15},{9,8},{10,9... | collective-permute-start | bytes 2068424 | tf_op jit(solution)/shard_map/ppermute | solution.py:61
  121.6 2.1 bitcast_dynamic-update-slice_fusion.5
  123.8 14.7 %collective-permute-done.2 = bf16[513,672]{1,0:T(8,128)(2,1)} collective-permute-done((bf16[513,672]{1,0:T(8,128)(2,1)S(1)}, bf16[513,672]{1,0:T(8,128)(2,1)}, u32[]{:S(2)}, u32[]{:S(2)}) %collective-permute-start.2) | collective-permute-done | bytes 689504 | tf_op jit(solution)/shard_map/ppermute | solution.py:61
  138.5 2.1 bitcast_dynamic-update-slice_fusion.4
  140.5 0.9 bitcast_dynamic-update-slice_fusion.3
  141.5 11.3 %collective-permute-done.4 = bf16[513,672]{1,0:T(8,128)(2,1)S(1)} collective-permute-done((bf16[513,672]{1,0:T(8,128)(2,1)S(1)}, bf16[513,672]{1,0:T(8,128)(2,1)S(1)}, u32[]{:S(2)}, u32[]{:S(2)}) %collective-permute-start.4) | collective-permute-done | bytes 689504 | tf_op jit(solution)/shard_map/ppermute | solution.py:61
  152.8 0.9 bitcast_dynamic-update-slice_fusion.2
  153.8 1.0 bitcast_dynamic-update-slice_fusion.1
  154.8 0.1 collective-permute-done.6
  154.8 0.9 bitcast_dynamic-update-slice_fusion
  155.8 6.6 %gather_fusion = bf16[8,513,672]{2,1,0:T(8,128)(2,1)} fusion(bf16[8,513,672]{2,1,0:T(8,128)(2,1)} %bitcast_dynamic-update-slice_fusion, s32[1024]{0:T(1024)S(1)} %pad_clamp_fusion), kind=kCustom, calls=%fused_computation | custom fusion | bytes 11031584 | tf_op jit(solution)/shard_map/jit(_take)/gather | solution.py:65
  162.3 3.5 %broadcast_select_fusion = bf16[8,513,672]{2,1,0:T(8,128)(2,1)S(1)} fusion(bf16[8,513,672]{2,1,0:T(8,128)(2,1)} %gather_fusion, pred[8]{0:T(512)(128)(4,1)S(1)} %compare_and_fusion), kind=kLoop, calls=%fused_computation.11 | loop fusion | flops 2757888 | bytes 11031560 | tf_op jit(solution)/shard_map/jit(_take)/select_n | solution.py:65
  165.9 1.4 fusion.1
  167.3 4.7 %fusion.3 = bf16[8,512,672]{2,1,0:T(8,128)(2,1)} fusion(f32[8,672]{1,0:T(8,128)S(1)} %bitcast.87, f32[512]{0:T(512)S(1)} %add_rsqrt_fusion.2, bf16[8,513,672]{2,1,0:T(8,128)(2,1)S(1)} %broadcast_select_fusion), kind=kLoop, calls=%fused_computation.6 | loop fusion | flops 11010048 | bytes 11033600 | tf_op jit(solution)/shard_map/convert_element_type | solution.py:70
  171.9 14.1 %all-gather.2.cloned.1.call-done = bf16[5376,1024]{1,0:T(8,128)(2,1)} async-done(((bf16[1344,1024]{1,0:T(8,128)(2,1)}), bf16[5376,1024]{1,0:T(8,128)(2,1)}) %all-gather.2.cloned.1.call-update) | async-done | bytes 11010064 | tf_op jit(solution)/shard_map/all_gather | solution.py:73
  186.1 8.3 %fusion.14 = f32[512,512]{0,1:T(8,128)S(1)} fusion(bf16[8,512,672]{2,1,0:T(8,128)(2,1)} %fusion.3, bf16[8,672,1024]{2,1,0:T(8,128)(2,1)} %bitcast.88), kind=kOutput, calls=%fused_computation.23 | convolution fusion | flops 2818572288 | bytes 12845056 | tf_op jit(solution)/shard_map/jrc,jcn->rn/dot_general | solution.py:80
  194.4 0.1 multiply_reduce_fusion.1
  194.5 0.1 multiply_multiply_fusion.1
  194.6 0.1 subtract_convert_fusion.1
  194.8 4.5 %collective-permute-start.7 = (bf16[512,512]{0,1:T(8,128)(2,1)S(1)}, bf16[512,512]{0,1:T(8,128)(2,1)S(1)}, u32[]{:S(2)}, u32[]{:S(2)}) collective-permute-start(bf16[512,512]{0,1:T(8,128)(2,1)S(1)} %pad_maximum_fusion.1), channel_id=1, source_target_pairs={{0,16},{8,24},{16,32},{24,40},{32,48},{40,56},{48,64},{56,72},{64,... | collective-permute-start | bytes 1572872 | tf_op jit(solution)/shard_map/ppermute | solution.py:26
  199.3 3.7 %collective-permute-start.8 = (bf16[512,512]{0,1:T(8,128)(2,1)S(1)}, bf16[512,512]{0,1:T(8,128)(2,1)S(1)}, u32[]{:S(2)}, u32[]{:S(2)}) collective-permute-start(bf16[512,512]{0,1:T(8,128)(2,1)S(1)} %pad_maximum_fusion.1), channel_id=1, source_target_pairs={{0,8},{8,16},{16,24},{24,32},{32,40},{40,48},{48,56},{56,64},{64,7... | collective-permute-start | bytes 1572872 | tf_op jit(solution)/shard_map/ppermute | solution.py:26
  203.0 5.5 %fusion.10 = f32[512,512,1]{0,1,2:T(8,128)S(1)} fusion(bf16[8,512,672]{2,1,0:T(8,128)(2,1)S(1)} %copy-done, bf16[8,672,1024]{2,1,0:T(8,128)(2,1)} %bitcast.89), kind=kOutput, calls=%fused_computation.17 | convolution fusion | flops 2818572288 | bytes 12058624 | tf_op jit(solution)/shard_map/jrc,jcn->rn/dot_general | solution.py:93
  208.5 0.1 multiply_reduce_fusion
  208.7 0.2 multiply_multiply_fusion
  208.9 0.2 subtract_convert_fusion
  209.1 15.8 %collective-permute-done.7 = bf16[512,512]{0,1:T(8,128)(2,1)S(1)} collective-permute-done((bf16[512,512]{0,1:T(8,128)(2,1)S(1)}, bf16[512,512]{0,1:T(8,128)(2,1)S(1)}, u32[]{:S(2)}, u32[]{:S(2)}) %collective-permute-start.7) | collective-permute-done | bytes 524320 | tf_op jit(solution)/shard_map/ppermute | solution.py:26
  224.9 10.8 %collective-permute-done.8 = bf16[512,512]{0,1:T(8,128)(2,1)S(1)} collective-permute-done((bf16[512,512]{0,1:T(8,128)(2,1)S(1)}, bf16[512,512]{0,1:T(8,128)(2,1)S(1)}, u32[]{:S(2)}, u32[]{:S(2)}) %collective-permute-start.8) | collective-permute-done | bytes 524320 | tf_op jit(solution)/shard_map/ppermute | solution.py:26
  235.7 0.1 maximum_maximum_fusion
  235.8 0.1 fusion.35
  235.9 8.5 %fusion.36 = (f32[2,2,512]{2,1,0:T(2,128)S(1)}, bf16[2,2,512,1536]{2,3,1,0:T(8,128)(2,1)}) fusion(pred[512,1536]{0,1:T(8,128)(4,1)S(1)} %copy-done.1, bf16[1536,2,128,1]{0,2,3,1:T(8,128)(2,1)S(1)} %bitcast.85, bf16[512,2,2,128]{0,3,2,1:T(8,128)(2,1)S(1)} %bitcast.86), kind=kOutput, calls=%fused_computation.81 | convolution fusion | flops 824182272 | bytes 8396800 | tf_op jit(solution)/shard_map/sub | solution.py:118
  244.4 3.8 %fusion.25 = bf16[512,2,2,128]{0,3,2,1:T(8,128)(2,1)S(1)} fusion(bf16[1536,2,128,1]{0,2,3,1:T(8,128)(2,1)S(1)} %bitcast.84, bf16[2,2,512,1536]{2,3,1,0:T(8,128)(2,1)} %get-tuple-element.16, f32[512,2,2]{0,2,1:T(2,128)S(1)} %bitcast.91), kind=kOutput, calls=%fused_computation.27 | convolution fusion | flops 805830656 | bytes 7610368 | tf_op jit(solution)/shard_map/kgts,skd->tkgd/dot_general | solution.py:121
  248.2 8.6 %convolution_convert_fusion = bf16[512,5376]{0,1:T(8,128)(2,1)} fusion(bf16[512,512]{0,1:T(8,128)(2,1)S(1)} %bitcast.90, bf16[512,5376]{1,0:T(8,128)(2,1)} %param.15), kind=kOutput, calls=%fused_computation.10 | convolution fusion | flops 2821324800 | bytes 11534336 | tf_op jit(solution)/shard_map/dot_general | solution.py:126
  256.8 42.5 %reduce-scatter.2.cloned.1.call-done = bf16[512,672]{0,1:T(8,128)(2,1)} async-done(((bf16[512,5376]{0,1:T(8,128)(2,1)}), bf16[512,672]{0,1:T(8,128)(2,1)}) %reduce-scatter.2.cloned.1.call-update) | async-done | bytes 688144 | tf_op jit(solution)/shard_map/reduce_scatter | solution.py:127
  (39 shorter events, 0.4 us)
Async XLA Ops:
  6.5 75.3 %copy-start.2 = (bf16[512,672]{0,1:T(8,128)(2,1)S(1)}, bf16[512,672]{0,1:T(8,128)(2,1)}, u32[]{:S(2)}) copy-start(bf16[512,672]{0,1:T(8,128)(2,1)} %param.8) | copy-start | bytes 2064388
  6.5 179.5 %all-gather.2.cloned.1.call-start = ((), (), s32[]{:S(2)}) async-start(), calls=%async_computation.2 | async-start | bytes 13762560 | tf_op jit(solution)/shard_map/all_gather | solution.py:73
  7.7 74.5 %copy-start.3 = (bf16[1,672]{1,0:T(2,128)(2,1)S(1)}, bf16[1,672]{1,0:T(2,128)(2,1)}, u32[]{:S(2)}) copy-start(bf16[1,672]{1,0:T(2,128)(2,1)} %param.9) | copy-start | bytes 4036
  8.0 84.3 %copy-start.4 = (bf16[1,128]{1,0:T(2,128)(2,1)S(1)}, bf16[1,128]{1,0:T(2,128)(2,1)}, u32[]{:S(2)}) copy-start(bf16[1,128]{1,0:T(2,128)(2,1)} %param.14) | copy-start | bytes 772
  8.0 84.3 %copy-start.5 = (bf16[1,128]{1,0:T(2,128)(2,1)S(1)}, bf16[1,128]{1,0:T(2,128)(2,1)}, u32[]{:S(2)}) copy-start(bf16[1,128]{1,0:T(2,128)(2,1)} %param.13) | copy-start | bytes 772
  81.8 217.6 %reduce-scatter.2.cloned.1.call-start = ((), (), s32[]{:S(2)}) async-start(), calls=%async_computation.3 | async-start | bytes 6193152 | tf_op jit(solution)/shard_map/reduce_scatter | solution.py:127
  82.2 20.8 %collective-permute-start = (bf16[513,672]{1,0:T(8,128)(2,1)S(1)}, bf16[513,672]{1,0:T(8,128)(2,1)}, u32[]{:S(2)}, u32[]{:S(2)}) collective-permute-start(bf16[513,672]{1,0:T(8,128)(2,1)S(1)} %pad_maximum_fusion), channel_id=1, source_target_pairs={{0,1},{1,2},{2,3},{3,4},{4,5},{5,6},{6,7},{7,0},{8,9},{9,10},{10,1... | collective-permute-start | bytes 2068424 | tf_op jit(solution)/shard_map/ppermute | solution.py:61
  82.3 24.6 %collective-permute-start.1 = (bf16[513,672]{1,0:T(8,128)(2,1)S(1)}, bf16[513,672]{1,0:T(8,128)(2,1)}, u32[]{:S(2)}, u32[]{:S(2)}) collective-permute-start(bf16[513,672]{1,0:T(8,128)(2,1)S(1)} %pad_maximum_fusion), channel_id=1, source_target_pairs={{0,2},{1,3},{2,4},{3,5},{4,6},{5,7},{6,0},{7,1},{8,10},{9,11},{10,... | collective-permute-start | bytes 2068424 | tf_op jit(solution)/shard_map/ppermute | solution.py:61
  83.9 54.6 %collective-permute-start.2 = (bf16[513,672]{1,0:T(8,128)(2,1)S(1)}, bf16[513,672]{1,0:T(8,128)(2,1)}, u32[]{:S(2)}, u32[]{:S(2)}) collective-permute-start(bf16[513,672]{1,0:T(8,128)(2,1)S(1)} %pad_maximum_fusion), channel_id=1, source_target_pairs={{0,3},{1,4},{2,5},{3,6},{4,7},{5,0},{6,1},{7,2},{8,11},{9,12},{10,... | collective-permute-start | bytes 2068424 | tf_op jit(solution)/shard_map/ppermute | solution.py:61
  86.1 54.4 %collective-permute-start.3 = (bf16[513,672]{1,0:T(8,128)(2,1)S(1)}, bf16[513,672]{1,0:T(8,128)(2,1)S(1)}, u32[]{:S(2)}, u32[]{:S(2)}) collective-permute-start(bf16[513,672]{1,0:T(8,128)(2,1)S(1)} %pad_maximum_fusion), channel_id=1, source_target_pairs={{0,4},{1,5},{2,6},{3,7},{4,0},{5,1},{6,2},{7,3},{8,12},{9,13},{10,... | collective-permute-start | bytes 2068424 | tf_op jit(solution)/shard_map/ppermute | solution.py:61
  88.0 64.9 %collective-permute-start.4 = (bf16[513,672]{1,0:T(8,128)(2,1)S(1)}, bf16[513,672]{1,0:T(8,128)(2,1)S(1)}, u32[]{:S(2)}, u32[]{:S(2)}) collective-permute-start(bf16[513,672]{1,0:T(8,128)(2,1)S(1)} %pad_maximum_fusion), channel_id=1, source_target_pairs={{0,5},{1,6},{2,7},{3,0},{4,1},{5,2},{6,3},{7,4},{8,13},{9,14},{10,... | collective-permute-start | bytes 2068424 | tf_op jit(solution)/shard_map/ppermute | solution.py:61
  103.0 50.8 %collective-permute-start.5 = (bf16[513,672]{1,0:T(8,128)(2,1)S(1)}, bf16[513,672]{1,0:T(8,128)(2,1)S(1)}, u32[]{:S(2)}, u32[]{:S(2)}) collective-permute-start(bf16[513,672]{1,0:T(8,128)(2,1)S(1)} %pad_maximum_fusion), channel_id=1, source_target_pairs={{0,6},{1,7},{2,0},{3,1},{4,2},{5,3},{6,4},{7,5},{8,14},{9,15},{10,... | collective-permute-start | bytes 2068424 | tf_op jit(solution)/shard_map/ppermute | solution.py:61
  106.9 47.9 %collective-permute-start.6 = (bf16[513,672]{1,0:T(8,128)(2,1)S(1)}, bf16[513,672]{1,0:T(8,128)(2,1)S(1)}, u32[]{:S(2)}, u32[]{:S(2)}) collective-permute-start(bf16[513,672]{1,0:T(8,128)(2,1)S(1)} %pad_maximum_fusion), channel_id=1, source_target_pairs={{0,7},{1,0},{2,1},{3,2},{4,3},{5,4},{6,5},{7,6},{8,15},{9,8},{10,9... | collective-permute-start | bytes 2068424 | tf_op jit(solution)/shard_map/ppermute | solution.py:61
  186.1 16.9 %copy-start = (bf16[8,512,672]{2,1,0:T(8,128)(2,1)S(1)}, bf16[8,512,672]{2,1,0:T(8,128)(2,1)}, u32[]{:S(2)}) copy-start(bf16[8,512,672]{2,1,0:T(8,128)(2,1)} %fusion.3) | copy-start | bytes 16515076
  194.8 30.0 %collective-permute-start.7 = (bf16[512,512]{0,1:T(8,128)(2,1)S(1)}, bf16[512,512]{0,1:T(8,128)(2,1)S(1)}, u32[]{:S(2)}, u32[]{:S(2)}) collective-permute-start(bf16[512,512]{0,1:T(8,128)(2,1)S(1)} %pad_maximum_fusion.1), channel_id=1, source_target_pairs={{0,16},{8,24},{16,32},{24,40},{32,48},{40,56},{48,64},{56,72},{64,... | collective-permute-start | bytes 1572872 | tf_op jit(solution)/shard_map/ppermute | solution.py:26
  199.3 36.4 %collective-permute-start.8 = (bf16[512,512]{0,1:T(8,128)(2,1)S(1)}, bf16[512,512]{0,1:T(8,128)(2,1)S(1)}, u32[]{:S(2)}, u32[]{:S(2)}) collective-permute-start(bf16[512,512]{0,1:T(8,128)(2,1)S(1)} %pad_maximum_fusion.1), channel_id=1, source_target_pairs={{0,8},{8,16},{16,24},{24,32},{32,40},{40,48},{48,56},{56,64},{64,7... | collective-permute-start | bytes 1572872 | tf_op jit(solution)/shard_map/ppermute | solution.py:26
  208.5 27.4 %copy-start.1 = (pred[512,1536]{0,1:T(8,128)(4,1)S(1)}, pred[512,1536]{0,1:T(8,128)(4,1)}, u32[]{:S(2)}) copy-start(pred[512,1536]{0,1:T(8,128)(4,1)} %and_and_fusion) | copy-start | bytes 2359300
Sparse Core Ops, SparseCore 0:
  81.9 104.0 all-gather.1
  257.0 42.3 reduce-scatter.1
